TPU v7x, 32 devices: a whole 2x2x4 slice. The times are simulated.
32 devices in a mesh: dp: 4 (over z), fsdp: 2 (over x), rows: 4 (over y, core).
Axes of the slice: x: 2, y: 2, z: 4, core: 2. Of those that a mesh axis runs over, the one named last changes fastest.
Arguments:
- feature_maps: bfloat16 [8, 16, 32, 1536], P(('dp', 'fsdp'), 'rows'), may hold values from -30 to 30
- dw_kernel: float32 [7, 7, 1536], replicated, may hold values from -0.875 to 0.875
- norm_gain: float32 [1536], replicated, may hold values from 0.5 to 1.5
- w_up: bfloat16 [1536, 6144], P(('dp', 'rows'), 'fsdp'), may hold values from -0.15625 to 0.15625
- w_down: bfloat16 [6144, 1536], P('fsdp', ('dp', 'rows')), may hold values from -0.078125 to 0.078125
- layer_scale: float32 [1536], replicated, may hold values from 0.3 to 1.5
- d_out: bfloat16 [8, 16, 32, 1536], P(('dp', 'fsdp'), 'rows'), may hold values from -20 to 20
Outputs:
- result: bfloat16 [8, 16, 32, 1536], P(('dp', 'fsdp'), 'rows')
- grad_x: bfloat16 [8, 16, 32, 1536], P(('dp', 'fsdp'), 'rows')
- grad_up: float32 [1536, 6144], P(('dp', 'rows'), 'fsdp')
- grad_down: float32 [6144, 1536], P('fsdp', ('dp', 'rows'))
- grad_kernel: float32 [7, 7, 1536], replicated
- grad_gain: float32 [1536], replicated
- grad_scale: float32 [1536], replicated
All inputs are finite; a program needn't handle non-finite values.
Results may differ from a plain program's by a relative error of at most 0.0075.
Values may be sent and summed in bfloat16 or wider, within the bound.
No kernel may reach another device: no remote copies, remote signals or barrier semaphores. Data moves between devices by JAX's collectives and lax.ppermute only.
A program may use at most 128 MiB of HBM per device.

v0:
```python
import math
import jax
import jax.numpy as jnp
from jax import lax
from jax.sharding import PartitionSpec as P

KS = 7
norm_eps = 1e-06
inv_root_two = 1.0 / math.sqrt(2.0)
inv_root_two_pi = 1.0 / math.sqrt(2.0 * math.pi)
contract_rows = (((0,), (0,)), ((), ()))
contract_cols = (((1,), (1,)), ((), ()))


def padded_2(x, sides, width):
    for axis, dim in sides:
        devices, length = (lax.axis_size(axis), x.shape[dim])
        up = [(i, (i + 1) % devices) for i in range(devices - 1)]
        down = [(j, i) for i, j in up]
        last = lax.slice_in_dim(x, length - width, length, axis=dim)
        leading = lax.slice_in_dim(x, 0, width, axis=dim)
        before = lax.ppermute(last, axis, up)
        after = lax.ppermute(leading, axis, down)
        x = jnp.concatenate([before, x, after], axis=dim)
    return x


def gelu_exact(values):
    return 0.5 * values * (1.0 + jax.scipy.special.erf(values * inv_root_two))


def gelu_slope(values):
    cdf_part = 0.5 * (1.0 + jax.scipy.special.erf(values * inv_root_two))
    return cdf_part + values * jnp.exp(-0.5 * values * values) * inv_root_two_pi


def body(feature_maps, dw_kernel, norm_gain, w_up, w_down, layer_scale, d_out):
    scenes, strip, across, width = feature_maps.shape
    cells = scenes * strip * across
    hid_axes = ("fsdp", "rows")
    up_loc = lax.all_to_all(w_up, "rows", 1, 0, tiled=True)
    up_loc = lax.all_gather(up_loc, "dp", axis=0, tiled=True)
    down_loc = lax.all_to_all(w_down, "rows", 0, 1, tiled=True)
    down_loc = lax.all_gather(down_loc, "dp", axis=1, tiled=True)
    cotan = d_out.reshape(cells, width).astype(jnp.float32)
    back = (cotan * layer_scale).astype(jnp.bfloat16)
    back_all = lax.all_gather(back, hid_axes, axis=0, tiled=True)
    rimmed = padded_2(feature_maps, (("rows", 1),), 3)
    padded = jnp.pad(rimmed.astype(jnp.float32), ((0, 0), (0, 0), (3, 3), (0, 0)))
    filtered = jnp.zeros(feature_maps.shape, jnp.float32)
    for row_off in range(KS):
        for col_off in range(KS):
            filtered = (
                filtered
                + padded[:, row_off : row_off + strip, col_off : col_off + across, :]
                * dw_kernel[row_off, col_off]
            )
    flat = filtered.reshape(cells, width)
    average = jnp.mean(flat, axis=-1, keepdims=True)
    center = flat - average
    variance = jnp.mean(center * center, axis=-1, keepdims=True)
    rstd = lax.rsqrt(variance + norm_eps)
    normed = center * rstd
    scaled = (normed * norm_gain).astype(jnp.bfloat16)
    gathered = lax.all_gather(scaled, hid_axes, axis=0, tiled=True)
    hidden = jnp.dot(gathered, up_loc, preferred_element_type=jnp.float32)
    active = gelu_exact(hidden).astype(jnp.bfloat16)
    mlp_terms = jnp.dot(active, down_loc, preferred_element_type=jnp.float32)
    branch = lax.psum_scatter(
        mlp_terms.astype(jnp.bfloat16), hid_axes, scatter_dimension=0, tiled=True
    ).astype(jnp.float32)
    resid = feature_maps.reshape(cells, width).astype(jnp.float32)
    result = (resid + layer_scale * branch).astype(jnp.bfloat16).reshape(feature_maps.shape)
    scale_part = jnp.sum(cotan * branch, axis=0)
    down_part = lax.dot_general(active, back_all, contract_rows, preferred_element_type=jnp.float32)
    slope_in = lax.dot_general(
        back_all, down_loc, contract_cols, preferred_element_type=jnp.float32
    )
    hidden_grad = (slope_in * gelu_slope(hidden)).astype(jnp.bfloat16)
    up_part = lax.dot_general(
        gathered, hidden_grad, contract_rows, preferred_element_type=jnp.float32
    )
    norm_terms = lax.dot_general(
        hidden_grad, up_loc, contract_cols, preferred_element_type=jnp.float32
    )
    norm_grad = lax.psum_scatter(norm_terms, hid_axes, scatter_dimension=0, tiled=True)
    grad_up = lax.psum_scatter(up_part, "dp", scatter_dimension=0, tiled=True)
    grad_up = lax.all_to_all(grad_up, "rows", 0, 1, tiled=True)
    grad_down = lax.psum_scatter(down_part, "dp", scatter_dimension=1, tiled=True)
    grad_down = lax.all_to_all(grad_down, "rows", 1, 0, tiled=True)
    gain_part = jnp.sum(norm_grad * normed, axis=0)
    scaled_grad = norm_grad * norm_gain
    conv_grad = rstd * (
        scaled_grad
        - jnp.mean(scaled_grad, axis=-1, keepdims=True)
        - normed * jnp.mean(scaled_grad * normed, axis=-1, keepdims=True)
    )
    conv_grad = conv_grad.reshape(feature_maps.shape)
    grad_rim = padded_2(conv_grad.astype(jnp.bfloat16), (("rows", 1),), 3).astype(conv_grad.dtype)
    grad_pad = jnp.pad(grad_rim, ((0, 0), (0, 0), (3, 3), (0, 0)))
    kernel_rows = []
    back_conv = jnp.zeros(feature_maps.shape, jnp.float32)
    for row_off in range(KS):
        for col_off in range(KS):
            window = padded[:, row_off : row_off + strip, col_off : col_off + across, :]
            kernel_rows.append(jnp.sum(window * conv_grad, axis=(0, 1, 2)))
            back_conv = (
                back_conv
                + grad_pad[
                    :, 6 - row_off : 6 - row_off + strip, 6 - col_off : 6 - col_off + across, :
                ]
                * dw_kernel[row_off, col_off]
            )
    kernel_part = jnp.stack(kernel_rows).reshape(KS, KS, width)
    grad_x = (d_out.astype(jnp.float32) + back_conv).astype(jnp.bfloat16)
    grad_kernel, grad_gain, grad_scale = lax.psum(
        (kernel_part, gain_part, scale_part), ("dp", "fsdp", "rows")
    )
    return (result, grad_x, grad_up, grad_down, grad_kernel, grad_gain, grad_scale)


def solution(mesh):
    return jax.shard_map(
        body,
        mesh=mesh,
        in_specs=(
            P(("dp", "fsdp"), "rows", None, None),
            P(),
            P(),
            P(("dp", "rows"), "fsdp"),
            P("fsdp", ("dp", "rows")),
            P(),
            P(("dp", "fsdp"), "rows", None, None),
        ),
        out_specs=(
            P(("dp", "fsdp"), "rows", None, None),
            P(("dp", "fsdp"), "rows", None, None),
            P(("dp", "rows"), "fsdp"),
            P("fsdp", ("dp", "rows")),
            P(),
            P(),
            P(),
        ),
        check_vma=False,
    )
```

profile of v0, /device:TPU:1, one launch (start us, length us, event | category | flops | bytes accessed | tf_op | source)
XLA Modules:
  0.0 634.2 jit_solution(6933835637550639418)
XLA Ops:
  7.2 1.2 copy.35
  8.4 13.0 %all_to_all.76 = bf16[96,4,768]{2,0,1:T(8,128)(2,1)} all-to-all(bf16[96,4,768]{2,0,1:T(8,128)(2,1)S(1)} %bitcast.112), channel_id=1, replica_groups=mesh['dp'=4,'fsdp'=2,'rows'=4] {'rows'}, dimensions={1} | all-to-all | bytes 1179648 | tf_op jit(solution)/shard_map/all_to_all | solution.py:41
  21.5 2.6 collective-permute-start
  24.2 1.9 collective-permute-start.1
  26.9 0.9 slice_reduce_fusion.47
  27.9 4.3 collective-permute-done.1
  32.4 9.5 %fusion.103 = (f32[4,32]{1,0:T(4,128)S(1)}, f32[1,4,32,1536]{3,2,1,0:T(8,128)S(1)}) fusion(f32[1536]{0:T(1024)S(1)} %get-tuple-element.106, f32[1536]{0:T(1024)S(1)} %get-tuple-element.107, f32[1536]{0:T(1024)S(1)} %get-tuple-element.60, f32[1536]{0:T(1024)S(1)} %get-tuple-element.61, f32[1,10,32,1536]{3,2,1,0:T(8,128)S(1)} %maximum_convert_fusion, ...), kind=kLoop, calls=%fused_computation.315 | loop fusion | flops 19267456 | bytes 8641024 | tf_op jit(solution)/shard_map/reduce_sum | solution.py:59
  42.6 0.9 multiply_convert_fusion.1
  43.6 1.1 copy.34
  44.7 10.7 %all_to_all.77 = bf16[4,768,96]{1,2,0:T(8,128)(2,1)} all-to-all(bf16[4,768,96]{1,2,0:T(8,128)(2,1)S(1)} %bitcast.113), channel_id=1, replica_groups=mesh['dp'=4,'fsdp'=2,'rows'=4] {'rows'}, dimensions={0} | all-to-all | bytes 1179648 | tf_op jit(solution)/shard_map/all_to_all | solution.py:43
  55.5 17.3 %all-gather.7.cloned.1.call-done = bf16[1536,768]{1,0:T(8,128)(2,1)} async-done(((bf16[384,768]{1,0:T(8,128)(2,1)}), bf16[1536,768]{1,0:T(8,128)(2,1)}) %all-gather.7.cloned.1.call-update) | async-done | bytes 2359312 | tf_op jit(solution)/shard_map/all_gather | solution.py:42
  72.8 34.1 %all-gather.5.cloned.1.call-done = bf16[1024,1536]{1,0:T(8,128)(2,1)} async-done(((bf16[128,1536]{1,0:T(8,128)(2,1)}), bf16[1024,1536]{1,0:T(8,128)(2,1)}) %all-gather.5.cloned.1.call-update) | async-done | bytes 3145744 | tf_op jit(solution)/shard_map/all_gather | solution.py:65
  106.9 7.4 %multiply_convert_fusion = (bf16[1024,768]{1,0:T(8,128)(2,1)}, f32[1024,768]{1,0:T(8,128)}) fusion(bf16[1024,1536]{1,0:T(8,128)(2,1)} %all-gather.5.cloned.1.call-done, bf16[1536,768]{1,0:T(8,128)(2,1)} %all-gather.7.cloned.1.call-done), kind=kOutput, calls=%fused_computation.92 | convolution fusion | flops 2419851264 | bytes 10223616 | tf_op jit(solution)/shard_map/dot_general | solution.py:66
  114.3 44.2 %all-gather.9.cloned.1.call-done = bf16[768,1536]{0,1:T(8,128)(2,1)} async-done(((bf16[768,384]{0,1:T(8,128)(2,1)}), bf16[768,1536]{0,1:T(8,128)(2,1)}) %all-gather.9.cloned.1.call-update) | async-done | bytes 2359312 | tf_op jit(solution)/shard_map/all_gather | solution.py:44
  158.5 6.5 %convolution_convert_fusion = bf16[1024,1536]{1,0:T(8,128)(2,1)} fusion(bf16[1024,768]{1,0:T(8,128)(2,1)} %get-tuple-element.120, bf16[768,1536]{0,1:T(8,128)(2,1)} %all-gather.9.cloned.1.call-done), kind=kOutput, calls=%fused_computation.85 | convolution fusion | flops 2417491968 | bytes 7077888 | tf_op jit(solution)/shard_map/dot_general | solution.py:68
  165.1 45.2 %reduce-scatter.5.cloned.1.call-done = bf16[128,1536]{1,0:T(8,128)(2,1)} async-done(((bf16[1024,1536]{1,0:T(8,128)(2,1)}), bf16[128,1536]{1,0:T(8,128)(2,1)}) %reduce-scatter.5.cloned.1.call-update) | async-done | bytes 393232 | tf_op jit(solution)/shard_map/reduce_scatter | solution.py:69
  210.2 2.7 fusion.8
  213.2 32.7 %all-gather.11.cloned.1.call-done = bf16[1024,1536]{1,0:T(8,128)(2,1)} async-done(((bf16[128,1536]{1,0:T(8,128)(2,1)}), bf16[1024,1536]{1,0:T(8,128)(2,1)}) %all-gather.11.cloned.1.call-update) | async-done | bytes 3145744 | tf_op jit(solution)/shard_map/all_gather | solution.py:47
  245.9 7.2 %fusion.108 = f32[768,1536]{1,0:T(8,128)} fusion(bf16[1024,768]{1,0:T(8,128)(2,1)} %get-tuple-element.120, bf16[1024,1536]{1,0:T(8,128)(2,1)} %all-gather.11.cloned.1.call-done), kind=kOutput, calls=%fused_computation.320 | convolution fusion | flops 2415919104 | bytes 9437184 | tf_op jit(solution)/shard_map/dot_general | solution.py:75
  253.1 6.8 %fusion.5 = bf16[1024,768]{1,0:T(8,128)(2,1)S(1)} fusion(f32[1024,768]{1,0:T(8,128)} %get-tuple-element.121, bf16[1024,1536]{1,0:T(8,128)(2,1)} %all-gather.11.cloned.1.call-done, bf16[768,1536]{0,1:T(8,128)(2,1)} %all-gather.9.cloned.1.call-done), kind=kOutput, calls=%fused_computation.91 | convolution fusion | flops 2423783424 | bytes 10223616 | tf_op jit(solution)/shard_map/dot_general | solution.py:76
  260.0 1.2 copy-done.49
  261.1 4.6 fusion.106
  265.8 7.2 %fusion.107 = f32[1536,768]{1,0:T(8,128)} fusion(bf16[1024,1536]{1,0:T(8,128)(2,1)} %all-gather.5.cloned.1.call-done, bf16[1024,768]{1,0:T(8,128)(2,1)} %copy-done.49), kind=kOutput, calls=%fused_computation.319 | convolution fusion | flops 2415919104 | bytes 9437184 | tf_op jit(solution)/shard_map/dot_general | solution.py:80
  273.0 65.1 %reduce-scatter.11.cloned.1.call-done = f32[768,384]{1,0:T(8,128)} async-done(((f32[768,1536]{1,0:T(8,128)}), f32[768,384]{1,0:T(8,128)}) %reduce-scatter.11.cloned.1.call-update) | async-done | bytes 1179664 | tf_op jit(solution)/shard_map/reduce_scatter | solution.py:89
  338.1 2.7 copy.26
  340.8 4.9 all-to-all-start.3
  345.7 58.4 %reduce-scatter.7.cloned.1.call-done = f32[128,1536]{1,0:T(8,128)} async-done(((f32[1024,1536]{1,0:T(8,128)}), f32[128,1536]{1,0:T(8,128)}) %reduce-scatter.7.cloned.1.call-update) | async-done | bytes 786448 | tf_op jit(solution)/shard_map/reduce_scatter | solution.py:86
  404.1 2.0 multiply_reduce_fusion
  406.2 3.6 multiply_reduce_fusion.2
  409.8 2.0 multiply_reduce_fusion.1
  411.8 0.9 fusion.104
  414.5 0.6 stack.172
  416.3 0.6 stack.176
  420.5 0.6 stack.184
  424.1 3.6 collective-permute-start.2
  427.7 1.9 collective-permute-start.3
  429.6 1.1 multiply_reduce_fusion.3
  431.2 4.2 stack.199
  435.4 0.8 reshape.335
  436.2 46.1 %all-reduce.2 = (f32[1536]{0:T(1024)}, f32[1536]{0:T(1024)}) all-reduce(f32[1536]{0:T(1024)} %get-tuple-element.56, f32[1536]{0:T(1024)} %get-tuple-element.113), channel_id=1, replica_groups=mesh['dp'=4,'fsdp'=2,'rows'=4] {'dp','fsdp','rows'}, use_global_device_ids=true, to_apply=%region_59.60 | all-reduce | flops 3072 | bytes 24576 | tf_op jit(solution)/shard_map/psum | solution.py:116
  482.4 10.4 %reduce-scatter.9.cloned.1.call-done = f32[384,768]{1,0:T(8,128)} async-done(((f32[1536,768]{1,0:T(8,128)}), f32[384,768]{1,0:T(8,128)}) %reduce-scatter.9.cloned.1.call-update) | async-done | bytes 1179664 | tf_op jit(solution)/shard_map/reduce_scatter | solution.py:87
  492.8 4.1 all-to-all-start.2
  496.9 8.0 %fusion.96 = bf16[1,4,32,1536]{3,2,1,0:T(8,128)(2,1)} fusion(f32[1,10,32,1536]{3,2,1,0:T(8,128)S(1)} %maximum_convert_fusion.1, bf16[1,4,32,1536]{3,2,1,0:T(8,128)(2,1)S(1)} %copy-done.1, f32[1536]{0:T(1024)} %copy-done.13, f32[1536]{0:T(1024)} %copy-done.14, f32[1536]{0:T(1024)} %copy-done.16, f32[1536]{0:T(1024)} %copy-done.17, f32[1536]{0:T(1024)} %copy-done.18, ...), kind=kLoop, calls=%fused_computation.188 | loop fusion | flops 19660800 | bytes 8562688 | tf_op jit(solution)/shard_map/convert_element_type | solution.py:115
  504.9 2.4 copy.31
  507.3 5.2 all-to-all-done.2
  512.5 1.1 copy.30
  513.7 112.3 %all-reduce.5.cloned.1.call-done = f32[7,7,1536]{2,1,0:T(8,128)} async-done(((f32[7,7,1536]{2,1,0:T(8,128)}), f32[7,7,1536]{2,1,0:T(8,128)}) %all-reduce.5.cloned.1.call-update) | async-done | bytes 301072 | tf_op jit(solution)/shard_map/psum | solution.py:116
  626.0 1.7 copy.37
  (180 shorter events, 11.9 us)
Async XLA Ops:
  7.2 18.9 %copy-start.2 = (f32[7,7,1536]{2,1,0:T(8,128)S(1)}, f32[7,7,1536]{2,1,0:T(8,128)}, u32[]{:S(2)}) copy-start(f32[7,7,1536]{2,1,0:T(8,128)} %param.8) | copy-start | bytes 903172
  7.2 65.6 %all-gather.7.cloned.1.call-start = ((), (), s32[]{:S(2)}) async-start(), calls=%async_computation.9 | async-start | bytes 2949120 | tf_op jit(solution)/shard_map/all_gather | solution.py:42
  21.4 85.5 %all-gather.5.cloned.1.call-start = ((), (), s32[]{:S(2)}) async-start(), calls=%async_computation.8 | async-start | bytes 3538944 | tf_op jit(solution)/shard_map/all_gather | solution.py:65
  21.5 6.3 %collective-permute-start = (bf16[1,3,32,1536]{3,2,1,0:T(8,128)(2,1)S(1)}, bf16[1,3,32,1536]{3,2,1,0:T(8,128)(2,1)S(1)}, u32[]{:S(2)}, u32[]{:S(2)}) collective-permute-start(bf16[1,3,32,1536]{3,2,1,0:T(8,128)(2,1)S(1)} %get-tuple-element.118), channel_id=1, source_target_pairs={{0,1},{1,2},{2,3},{4,5},{5,6},{6,7},{8,9},{9,10},{10,11},{12,13},{... | collective-permute-start | bytes 884744 | tf_op jit(solution)/shard_map/ppermute | solution.py:22
  24.2 8.0 %collective-permute-start.1 = (bf16[1,3,32,1536]{3,2,1,0:T(8,128)(2,1)S(1)}, bf16[1,3,32,1536]{3,2,1,0:T(8,128)(2,1)S(1)}, u32[]{:S(2)}, u32[]{:S(2)}) collective-permute-start(bf16[1,3,32,1536]{3,2,1,0:T(8,128)(2,1)S(1)} %get-tuple-element.119), channel_id=1, source_target_pairs={{1,0},{2,1},{3,2},{5,4},{6,5},{7,6},{9,8},{10,9},{11,10},{13,12},{... | collective-permute-start | bytes 884744 | tf_op jit(solution)/shard_map/ppermute | solution.py:23
  26.3 15.5 %copy-start.4 = (f32[1536]{0:T(1024)}, f32[1536]{0:T(1024)S(1)}, u32[]{:S(2)}) copy-start(f32[1536]{0:T(1024)S(1)} %get-tuple-element.98) | copy-start | bytes 18436
  26.3 15.5 %copy-start.6 = (f32[1536]{0:T(1024)}, f32[1536]{0:T(1024)S(1)}, u32[]{:S(2)}) copy-start(f32[1536]{0:T(1024)S(1)} %get-tuple-element.99) | copy-start | bytes 18436
  26.3 15.5 %copy-start.7 = (f32[1536]{0:T(1024)}, f32[1536]{0:T(1024)S(1)}, u32[]{:S(2)}) copy-start(f32[1536]{0:T(1024)S(1)} %get-tuple-element.100) | copy-start | bytes 18436
  26.3 15.5 %copy-start.8 = (f32[1536]{0:T(1024)}, f32[1536]{0:T(1024)S(1)}, u32[]{:S(2)}) copy-start(f32[1536]{0:T(1024)S(1)} %get-tuple-element.101) | copy-start | bytes 18436
  26.3 15.5 %copy-start.9 = (f32[1536]{0:T(1024)}, f32[1536]{0:T(1024)S(1)}, u32[]{:S(2)}) copy-start(f32[1536]{0:T(1024)S(1)} %get-tuple-element.102) | copy-start | bytes 18436
  26.3 15.5 %copy-start.10 = (f32[1536]{0:T(1024)}, f32[1536]{0:T(1024)S(1)}, u32[]{:S(2)}) copy-start(f32[1536]{0:T(1024)S(1)} %get-tuple-element.103) | copy-start | bytes 18436
  26.4 15.5 %copy-start.11 = (f32[1536]{0:T(1024)}, f32[1536]{0:T(1024)S(1)}, u32[]{:S(2)}) copy-start(f32[1536]{0:T(1024)S(1)} %get-tuple-element.104) | copy-start | bytes 18436
  26.4 15.5 %copy-start.12 = (f32[1536]{0:T(1024)}, f32[1536]{0:T(1024)S(1)}, u32[]{:S(2)}) copy-start(f32[1536]{0:T(1024)S(1)} %get-tuple-element.105) | copy-start | bytes 18436
  26.4 15.5 %copy-start.13 = (f32[1536]{0:T(1024)}, f32[1536]{0:T(1024)S(1)}, u32[]{:S(2)}) copy-start(f32[1536]{0:T(1024)S(1)} %get-tuple-element.106) | copy-start | bytes 18436
  26.4 15.5 %copy-start.14 = (f32[1536]{0:T(1024)}, f32[1536]{0:T(1024)S(1)}, u32[]{:S(2)}) copy-start(f32[1536]{0:T(1024)S(1)} %get-tuple-element.107) | copy-start | bytes 18436
  26.7 15.2 %copy-start.15 = (f32[1536]{0:T(1024)}, f32[1536]{0:T(1024)S(1)}, u32[]{:S(2)}) copy-start(f32[1536]{0:T(1024)S(1)} %get-tuple-element.59) | copy-start | bytes 18436
  26.7 15.2 %copy-start.16 = (f32[1536]{0:T(1024)}, f32[1536]{0:T(1024)S(1)}, u32[]{:S(2)}) copy-start(f32[1536]{0:T(1024)S(1)} %get-tuple-element.60) | copy-start | bytes 18436
  26.7 15.2 %copy-start.17 = (f32[1536]{0:T(1024)}, f32[1536]{0:T(1024)S(1)}, u32[]{:S(2)}) copy-start(f32[1536]{0:T(1024)S(1)} %get-tuple-element.61) | copy-start | bytes 18436
  26.7 15.2 %copy-start.18 = (f32[1536]{0:T(1024)}, f32[1536]{0:T(1024)S(1)}, u32[]{:S(2)}) copy-start(f32[1536]{0:T(1024)S(1)} %get-tuple-element.62) | copy-start | bytes 18436
  26.8 15.2 %copy-start.19 = (f32[1536]{0:T(1024)}, f32[1536]{0:T(1024)S(1)}, u32[]{:S(2)}) copy-start(f32[1536]{0:T(1024)S(1)} %get-tuple-element.63) | copy-start | bytes 18436
  26.8 15.2 %copy-start.20 = (f32[1536]{0:T(1024)}, f32[1536]{0:T(1024)S(1)}, u32[]{:S(2)}) copy-start(f32[1536]{0:T(1024)S(1)} %get-tuple-element.64) | copy-start | bytes 18436
  26.8 15.2 %copy-start.21 = (f32[1536]{0:T(1024)}, f32[1536]{0:T(1024)S(1)}, u32[]{:S(2)}) copy-start(f32[1536]{0:T(1024)S(1)} %get-tuple-element.65) | copy-start | bytes 18436
  26.8 15.2 %copy-start.22 = (f32[1536]{0:T(1024)}, f32[1536]{0:T(1024)S(1)}, u32[]{:S(2)}) copy-start(f32[1536]{0:T(1024)S(1)} %get-tuple-element.66) | copy-start | bytes 18436
  26.8 15.2 %copy-start.23 = (f32[1536]{0:T(1024)}, f32[1536]{0:T(1024)S(1)}, u32[]{:S(2)}) copy-start(f32[1536]{0:T(1024)S(1)} %get-tuple-element.67) | copy-start | bytes 18436
  26.8 15.2 %copy-start.24 = (f32[1536]{0:T(1024)}, f32[1536]{0:T(1024)S(1)}, u32[]{:S(2)}) copy-start(f32[1536]{0:T(1024)S(1)} %get-tuple-element.68) | copy-start | bytes 18436
  26.8 15.2 %copy-start.25 = (f32[1536]{0:T(1024)}, f32[1536]{0:T(1024)S(1)}, u32[]{:S(2)}) copy-start(f32[1536]{0:T(1024)S(1)} %get-tuple-element.69) | copy-start | bytes 18436
  26.8 15.2 %copy-start.26 = (f32[1536]{0:T(1024)}, f32[1536]{0:T(1024)S(1)}, u32[]{:S(2)}) copy-start(f32[1536]{0:T(1024)S(1)} %get-tuple-element.70) | copy-start | bytes 18436
  26.8 15.2 %copy-start.27 = (f32[1536]{0:T(1024)}, f32[1536]{0:T(1024)S(1)}, u32[]{:S(2)}) copy-start(f32[1536]{0:T(1024)S(1)} %get-tuple-element.71) | copy-start | bytes 18436
  26.8 15.2 %copy-start.28 = (f32[1536]{0:T(1024)}, f32[1536]{0:T(1024)S(1)}, u32[]{:S(2)}) copy-start(f32[1536]{0:T(1024)S(1)} %get-tuple-element.72) | copy-start | bytes 18436
  26.9 15.2 %copy-start.29 = (f32[1536]{0:T(1024)}, f32[1536]{0:T(1024)S(1)}, u32[]{:S(2)}) copy-start(f32[1536]{0:T(1024)S(1)} %get-tuple-element.73) | copy-start | bytes 18436
  26.9 15.2 %copy-start.30 = (f32[1536]{0:T(1024)}, f32[1536]{0:T(1024)S(1)}, u32[]{:S(2)}) copy-start(f32[1536]{0:T(1024)S(1)} %get-tuple-element.74) | copy-start | bytes 18436
  26.9 15.2 %copy-start.31 = (f32[1536]{0:T(1024)}, f32[1536]{0:T(1024)S(1)}, u32[]{:S(2)}) copy-start(f32[1536]{0:T(1024)S(1)} %get-tuple-element.75) | copy-start | bytes 18436
  26.9 15.2 %copy-start.32 = (f32[1536]{0:T(1024)}, f32[1536]{0:T(1024)S(1)}, u32[]{:S(2)}) copy-start(f32[1536]{0:T(1024)S(1)} %get-tuple-element.76) | copy-start | bytes 18436
  42.6 71.7 %copy-start.46 = (f32[128]{0:T(128)}, f32[128]{0:T(128)S(1)}, u32[]{:S(2)}) copy-start(f32[128]{0:T(128)S(1)} %rsqrt.12) | copy-start | bytes 1540
  43.6 114.9 %all-gather.9.cloned.1.call-start = ((), (), s32[]{:S(2)}) async-start(), calls=%async_computation.10 | async-start | bytes 2949120 | tf_op jit(solution)/shard_map/all_gather | solution.py:44
  55.4 154.8 %reduce-scatter.5.cloned.1.call-start = ((), (), s32[]{:S(2)}) async-start(), calls=%async_computation.11 | async-start | bytes 3538944 | tf_op jit(solution)/shard_map/reduce_scatter | solution.py:69
  165.0 45.2 %copy-start.1 = (bf16[1,4,32,1536]{3,2,1,0:T(8,128)(2,1)S(1)}, bf16[1,4,32,1536]{3,2,1,0:T(8,128)(2,1)}, u32[]{:S(2)}) copy-start(bf16[1,4,32,1536]{3,2,1,0:T(8,128)(2,1)} %param.13) | copy-start | bytes 1179652
  165.0 80.8 %all-gather.11.cloned.1.call-start = ((), (), s32[]{:S(2)}) async-start(), calls=%async_computation.12 | async-start | bytes 3538944 | tf_op jit(solution)/shard_map/all_gather | solution.py:47
  213.0 125.2 %reduce-scatter.11.cloned.1.call-start = ((), (), s32[]{:S(2)}) async-start(), calls=%async_computation.15 | async-start | bytes 5898240 | tf_op jit(solution)/shard_map/reduce_scatter | solution.py:89
  253.1 151.0 %reduce-scatter.7.cloned.1.call-start = ((), (), s32[]{:S(2)}) async-start(), calls=%async_computation.13 | async-start | bytes 7077888 | tf_op jit(solution)/shard_map/reduce_scatter | solution.py:86
  265.7 227.1 %reduce-scatter.9.cloned.1.call-start = ((), (), s32[]{:S(2)}) async-start(), calls=%async_computation.14 | async-start | bytes 5898240 | tf_op jit(solution)/shard_map/reduce_scatter | solution.py:87
  273.0 131.1 %copy-start.45 = (f32[128]{0:T(128)S(1)}, f32[128]{0:T(128)}, u32[]{:S(2)}) copy-start(f32[128]{0:T(128)} %copy-done.44) | copy-start | bytes 1540
  273.0 131.1 %copy-start.47 = (f32[128]{0:T(128)S(1)}, f32[128]{0:T(128)}, u32[]{:S(2)}) copy-start(f32[128]{0:T(128)} %copy-done.46) | copy-start | bytes 1540
  340.8 152.0 %all-to-all-start.3 = ((f32[768,4,96]{0,2,1:T(8,128)}), f32[768,4,96]{0,2,1:T(8,128)}, u32[]{:S(2)}, u32[]{:S(2)}) async-start(f32[768,4,96]{0,2,1:T(8,128)} %bitcast.108), calls=%async_computation.7 | async-start | bytes 2359296 | tf_op jit(solution)/shard_map/all_to_all | solution.py:90
  345.7 280.3 %all-reduce.5.cloned.1.call-start = ((), (), s32[]{:S(2)}) async-start(), calls=%async_computation.16 | async-start | bytes 688128 | tf_op jit(solution)/shard_map/psum | solution.py:116
  424.1 58.2 %collective-permute-start.2 = (bf16[1,3,32,1536]{3,2,1,0:T(8,128)(2,1)}, bf16[1,3,32,1536]{3,2,1,0:T(8,128)(2,1)S(1)}, u32[]{:S(2)}, u32[]{:S(2)}) collective-permute-start(bf16[1,3,32,1536]{3,2,1,0:T(8,128)(2,1)} %get-tuple-element.116), channel_id=1, source_target_pairs={{0,1},{1,2},{2,3},{4,5},{5,6},{6,7},{8,9},{9,10},{10,11},{12,13},{... | collective-permute-start | bytes 884744 | tf_op jit(solution)/shard_map/ppermute | solution.py:22
  427.7 54.6 %collective-permute-start.3 = (bf16[1,3,32,1536]{3,2,1,0:T(8,128)(2,1)}, bf16[1,3,32,1536]{3,2,1,0:T(8,128)(2,1)S(1)}, u32[]{:S(2)}, u32[]{:S(2)}) collective-permute-start(bf16[1,3,32,1536]{3,2,1,0:T(8,128)(2,1)} %get-tuple-element.117), channel_id=1, source_target_pairs={{1,0},{2,1},{3,2},{5,4},{6,5},{7,6},{9,8},{10,9},{11,10},{13,12},{... | collective-permute-start | bytes 884744 | tf_op jit(solution)/shard_map/ppermute | solution.py:23
  492.8 19.8 %all-to-all-start.2 = ((f32[4,96,768]{2,1,0:T(8,128)}), f32[4,96,768]{2,1,0:T(8,128)S(1)}, u32[]{:S(2)}, u32[]{:S(2)}) async-start(f32[4,96,768]{2,1,0:T(8,128)} %bitcast.115), calls=%async_computation.5 | async-start | bytes 2359296 | tf_op jit(solution)/shard_map/all_to_all | solution.py:88
  (17 other events, 220.0 us)
Sparse Core Ops, SparseCore 0:
  21.5 51.2 all-gather.6
  75.3 31.5 all-gather.4
  108.5 50.0 all-gather.8
  165.1 45.0 reduce-scatter.4
  213.1 32.7 all-gather.10
  253.2 84.8 reduce-scatter.10
  341.9 62.1 reduce-scatter.6
  406.4 86.3 reduce-scatter.8
  498.7 127.2 all-reduce.4
where the time goes:
time: 635 us; the launch traced here: 634 us
  waiting for transfers between devices  429 us (68%)
  blocking collectives  69.8 us (11%)
  matrix products  39.7 us (6%)
  local copies, waits for them, and re-layouts  30.5 us (5%)
  other arithmetic  30.4 us (5%)
  starting transfers between devices  19.6 us (3%)
  between operations  14.9 us (2%)
    psum x1, waiting for transfers between devices, body(): lax.psum((kernel_part, gain_part, scale_part), ('dp', 'fsdp', 'rows'))  112 us
    reduce_scatter x1, waiting for transfers between devices, body(): lax.psum_scatter(down_part, 'dp', scatter_dimension=1, tiled=True)  65.1 us
    reduce_scatter x1, waiting for transfers between devices, body(): lax.psum_scatter(norm_terms, hid_axes, scatter_dimension=0, tiled=True)  58.4 us
    psum x1, blocking collectives, body(): lax.psum((kernel_part, gain_part, scale_part), ('dp', 'fsdp', 'rows'))  46.1 us
    reduce_scatter x1, waiting for transfers between devices, body(): lax.psum_scatter(mlp_terms.astype(jnp.bfloat16), hid_axes, scatter_dimens...  45.2 us
    all_gather x1, waiting for transfers between devices, body(): down_loc = lax.all_gather(down_loc, 'dp', axis=1, tiled=True)  44.2 us
    all_gather x1, waiting for transfers between devices, body(): gathered = lax.all_gather(scaled, hid_axes, axis=0, tiled=True)  34.1 us
    all_gather x1, waiting for transfers between devices, body(): back_all = lax.all_gather(back, hid_axes, axis=0, tiled=True)  32.7 us
  transfers between devices with their start and end apart: 15, of which 11 were waited for; matrix products, arithmetic and copies ran while one was open for 13% of the time, Pallas kernels for 0%

commit v1 on v0

--- a/solution.py
+++ b/solution.py
@@ -41,7 +41,12 @@
     up_loc = lax.all_to_all(w_up, "rows", 1, 0, tiled=True)
     up_loc = lax.all_gather(up_loc, "dp", axis=0, tiled=True)
     down_loc = lax.all_to_all(w_down, "rows", 0, 1, tiled=True)
-    down_loc = lax.all_gather(down_loc, "dp", axis=1, tiled=True)
+    ring = [down_loc]
+    for hop in range(3):
+        ring.append(lax.ppermute(ring[-1], "dp", [(dev, (dev + 1) % 4) for dev in range(4)]))
+    down_loc = jnp.roll(
+        jnp.concatenate(ring[::-1], axis=1), (lax.axis_index("dp") + 1) * ring[0].shape[1], axis=1
+    )
     cotan = d_out.reshape(cells, width).astype(jnp.float32)
     back = (cotan * layer_scale).astype(jnp.bfloat16)
     back_all = lax.all_gather(back, hid_axes, axis=0, tiled=True)

time: 635 us -> 613 us (0.965)
  waiting for transfers between devices: 429 us -> 393 us
  local copies, waits for them, and re-layouts: 30.5 us -> 41.4 us
    ppermute x0 -> x3, waiting for transfers between devices: none -> 59.4 us  [body(): lax.ppermute(ring[-1], 'dp', [(dev, (dev + 1) % 4) for dev in range(4)])]
    all_gather x1 -> x0, waiting for transfers between devices: 44.2 us -> none  [body(): down_loc = lax.all_gather(down_loc, 'dp', axis=1, tiled=True)]
    all_gather x1, waiting for transfers between devices: 34.1 us -> 0.01 us  [body(): gathered = lax.all_gather(scaled, hid_axes, axis=0, tiled=True)]
    all_gather x1, waiting for transfers between devices: 17.3 us -> 0.01 us  [body(): up_loc = lax.all_gather(up_loc, 'dp', axis=0, tiled=True)]
    unnamed x101 -> x116, local copies, waits for them, and re-layouts: 3.09 us -> 14.2 us
  transfers between devices with their start and end apart: 15 -> 17, of which waited for: 11 -> 11; matrix products, arithmetic and copies ran while one was open for 13% -> 14% of each run, Pallas kernels for 0% -> 0%
where the time goes in v1:
time: 613 us; the launch traced here: 612 us
  waiting for transfers between devices  393 us (64%)
  blocking collectives  69.8 us (11%)
  local copies, waits for them, and re-layouts  41.4 us (7%)
  matrix products  39.9 us (7%)
  other arithmetic  31.4 us (5%)
  starting transfers between devices  21.2 us (3%)
  between operations  15.2 us (2%)
    psum x1, waiting for transfers between devices, body(): lax.psum((kernel_part, gain_part, scale_part), ('dp', 'fsdp', 'rows'))  112 us
    reduce_scatter x1, waiting for transfers between devices, body(): lax.psum_scatter(down_part, 'dp', scatter_dimension=1, tiled=True)  64.9 us
    ppermute x3, waiting for transfers between devices, body(): lax.ppermute(ring[-1], 'dp', [(dev, (dev + 1) % 4) for dev in range(4)])  59.4 us
    reduce_scatter x1, waiting for transfers between devices, body(): lax.psum_scatter(norm_terms, hid_axes, scatter_dimension=0, tiled=True)  58.3 us
    reduce_scatter x1, waiting for transfers between devices, body(): lax.psum_scatter(mlp_terms.astype(jnp.bfloat16), hid_axes, scatter_dimens...  46.5 us
    psum x1, blocking collectives, body(): lax.psum((kernel_part, gain_part, scale_part), ('dp', 'fsdp', 'rows'))  46.1 us
    all_gather x1, waiting for transfers between devices, body(): back_all = lax.all_gather(back, hid_axes, axis=0, tiled=True)  32.6 us
    another operation x50, local copies, waits for them, and re-layouts, body(): kernel_part = jnp.stack(kernel_rows).reshape(KS, KS, width)  15.7 us
  transfers between devices with their start and end apart: 17, of which 11 were waited for; matrix products, arithmetic and copies ran while one was open for 14% of the time, Pallas kernels for 0%

profile of v1, /device:TPU:1, one launch (start us, length us, event | category | flops | bytes accessed | tf_op | source)
XLA Modules:
  0.0 612.0 jit_solution(3413248072680261961)
XLA Ops:
  7.2 1.2 copy.35
  8.4 13.0 %all_to_all.76 = bf16[96,4,768]{2,0,1:T(8,128)(2,1)} all-to-all(bf16[96,4,768]{2,0,1:T(8,128)(2,1)S(1)} %bitcast.112), channel_id=1, replica_groups=mesh['dp'=4,'fsdp'=2,'rows'=4] {'rows'}, dimensions={1} | all-to-all | bytes 1179648 | tf_op jit(solution)/shard_map/all_to_all | solution.py:41
  21.5 2.6 collective-permute-start
  24.2 1.9 collective-permute-start.1
  26.9 0.9 slice_reduce_fusion.47
  27.9 4.3 collective-permute-done.1
  32.8 9.4 %fusion.110 = (f32[4,32]{1,0:T(4,128)S(1)}, f32[1,4,32,1536]{3,2,1,0:T(8,128)S(1)}) fusion(f32[1536]{0:T(1024)S(1)} %get-tuple-element.106, f32[1536]{0:T(1024)S(1)} %get-tuple-element.107, f32[1536]{0:T(1024)S(1)} %get-tuple-element.60, f32[1536]{0:T(1024)S(1)} %get-tuple-element.61, f32[1,10,32,1536]{3,2,1,0:T(8,128)S(1)} %maximum_convert_fusion, ...), kind=kLoop, calls=%fused_computation.328 | loop fusion | flops 19267456 | bytes 8641024 | tf_op jit(solution)/shard_map/reduce_sum | solution.py:64
  42.6 0.9 multiply_convert_fusion.1
  43.7 10.7 %all_to_all.77 = bf16[4,768,96]{1,2,0:T(8,128)(2,1)S(1)} all-to-all(bf16[4,768,96]{1,2,0:T(8,128)(2,1)S(1)} %bitcast.113), channel_id=1, replica_groups=mesh['dp'=4,'fsdp'=2,'rows'=4] {'rows'}, dimensions={0} | all-to-all | bytes 1179648 | tf_op jit(solution)/shard_map/all_to_all | solution.py:43
  54.4 1.7 collective-permute-start.2
  56.1 28.7 %collective-permute-done.2 = bf16[768,384]{0,1:T(8,128)(2,1)S(1)} collective-permute-done((bf16[768,384]{0,1:T(8,128)(2,1)S(1)}, bf16[768,384]{0,1:T(8,128)(2,1)S(1)}, u32[]{:S(2)}, u32[]{:S(2)}) %collective-permute-start.2) | collective-permute-done | bytes 589856 | tf_op jit(solution)/shard_map/ppermute | solution.py:46
  85.6 15.7 %collective-permute-done.3 = bf16[768,384]{0,1:T(8,128)(2,1)} collective-permute-done((bf16[768,384]{0,1:T(8,128)(2,1)S(1)}, bf16[768,384]{0,1:T(8,128)(2,1)}, u32[]{:S(2)}, u32[]{:S(2)}) %collective-permute-start.3) | collective-permute-done | bytes 589856 | tf_op jit(solution)/shard_map/ppermute | solution.py:46
  101.3 15.0 %collective-permute-done.4 = bf16[768,384]{0,1:T(8,128)(2,1)} collective-permute-done((bf16[768,384]{0,1:T(8,128)(2,1)}, bf16[768,384]{0,1:T(8,128)(2,1)}, u32[]{:S(2)}, u32[]{:S(2)}) %collective-permute-start.4) | collective-permute-done | bytes 589856 | tf_op jit(solution)/shard_map/ppermute | solution.py:46
  116.3 1.9 constant_dynamic-update-slice_fusion.7
  118.2 1.9 constant_dynamic-update-slice_fusion.6
  121.9 1.9 constant_dynamic-update-slice_fusion.3
  123.8 1.9 constant_dynamic-update-slice_fusion.2
  127.4 7.4 %multiply_convert_fusion = (bf16[1024,768]{1,0:T(8,128)(2,1)}, f32[1024,768]{1,0:T(8,128)}) fusion(bf16[1024,1536]{1,0:T(8,128)(2,1)} %all-gather.4.cloned.1.call-done, bf16[1536,768]{1,0:T(8,128)(2,1)} %all-gather.6.cloned.1.call-done), kind=kOutput, calls=%fused_computation.92 | convolution fusion | flops 2419851264 | bytes 10223616 | tf_op jit(solution)/shard_map/dot_general | solution.py:71
  134.8 6.5 %convolution_convert_fusion = bf16[1024,1536]{1,0:T(8,128)(2,1)} fusion(bf16[1024,768]{1,0:T(8,128)(2,1)} %get-tuple-element.120, bf16[768,3072]{0,1:T(8,128)(2,1)} %constant_dynamic-update-slice_fusion, s32[]{:T(128)S(6)} %select_n.14), kind=kOutput, calls=%fused_computation.85 | convolution fusion | flops 2417491968 | bytes 7077892 | tf_op jit(solution)/shard_map/dot_general | solution.py:73
  141.4 46.5 %reduce-scatter.5.cloned.1.call-done = bf16[128,1536]{1,0:T(8,128)(2,1)} async-done(((bf16[1024,1536]{1,0:T(8,128)(2,1)}), bf16[128,1536]{1,0:T(8,128)(2,1)}) %reduce-scatter.5.cloned.1.call-update) | async-done | bytes 393232 | tf_op jit(solution)/shard_map/reduce_scatter | solution.py:74
  187.9 2.7 fusion.13
  190.9 32.6 %all-gather.8.cloned.1.call-done = bf16[1024,1536]{1,0:T(8,128)(2,1)} async-done(((bf16[128,1536]{1,0:T(8,128)(2,1)}), bf16[1024,1536]{1,0:T(8,128)(2,1)}) %all-gather.8.cloned.1.call-update) | async-done | bytes 3145744 | tf_op jit(solution)/shard_map/all_gather | solution.py:52
  223.5 7.2 %fusion.115 = f32[768,1536]{1,0:T(8,128)} fusion(bf16[1024,768]{1,0:T(8,128)(2,1)} %get-tuple-element.120, bf16[1024,1536]{1,0:T(8,128)(2,1)} %all-gather.8.cloned.1.call-done), kind=kOutput, calls=%fused_computation.333 | convolution fusion | flops 2415919104 | bytes 9437184 | tf_op jit(solution)/shard_map/dot_general | solution.py:80
  230.8 6.9 %fusion.5 = bf16[1024,768]{1,0:T(8,128)(2,1)S(1)} fusion(f32[1024,768]{1,0:T(8,128)} %get-tuple-element.121, bf16[1024,1536]{1,0:T(8,128)(2,1)} %all-gather.8.cloned.1.call-done, bf16[768,3072]{0,1:T(8,128)(2,1)} %constant_dynamic-update-slice_fusion, s32[]{:T(128)S(6)} %select_n.14), kind=kOutput, calls=%fused_computation.91 | convolution fusion | flops 2423783424 | bytes 10223620 | tf_op jit(solution)/shard_map/dot_general | solution.py:81
  237.7 1.2 copy-done.53
  238.9 4.6 fusion.113
  243.5 7.2 %fusion.114 = f32[1536,768]{1,0:T(8,128)} fusion(bf16[1024,1536]{1,0:T(8,128)(2,1)} %all-gather.4.cloned.1.call-done, bf16[1024,768]{1,0:T(8,128)(2,1)} %copy-done.53), kind=kOutput, calls=%fused_computation.332 | convolution fusion | flops 2415919104 | bytes 9437184 | tf_op jit(solution)/shard_map/dot_general | solution.py:85
  250.8 64.9 %reduce-scatter.11.cloned.1.call-done = f32[768,384]{1,0:T(8,128)} async-done(((f32[768,1536]{1,0:T(8,128)}), f32[768,384]{1,0:T(8,128)}) %reduce-scatter.11.cloned.1.call-update) | async-done | bytes 1179664 | tf_op jit(solution)/shard_map/reduce_scatter | solution.py:94
  315.8 2.7 copy.26
  318.4 4.9 all-to-all-start.3
  323.3 58.3 %reduce-scatter.7.cloned.1.call-done = f32[128,1536]{1,0:T(8,128)} async-done(((f32[1024,1536]{1,0:T(8,128)}), f32[128,1536]{1,0:T(8,128)}) %reduce-scatter.7.cloned.1.call-update) | async-done | bytes 786448 | tf_op jit(solution)/shard_map/reduce_scatter | solution.py:91
  381.6 2.0 multiply_reduce_fusion
  383.7 3.6 multiply_reduce_fusion.2
  387.3 2.0 multiply_reduce_fusion.1
  401.6 3.6 collective-permute-start.5
  405.2 1.9 collective-permute-start.6
  407.1 1.1 multiply_reduce_fusion.3
  408.7 4.2 stack.199
  413.7 46.1 %all-reduce.2 = (f32[1536]{0:T(1024)}, f32[1536]{0:T(1024)}) all-reduce(f32[1536]{0:T(1024)} %get-tuple-element.56, f32[1536]{0:T(1024)} %get-tuple-element.113), channel_id=1, replica_groups=mesh['dp'=4,'fsdp'=2,'rows'=4] {'dp','fsdp','rows'}, use_global_device_ids=true, to_apply=%region_59.60 | all-reduce | flops 3072 | bytes 24576 | tf_op jit(solution)/shard_map/psum | solution.py:121
  459.8 1.1 maximum_convert_fusion.1
  460.9 9.4 %reduce-scatter.9.cloned.1.call-done = f32[384,768]{1,0:T(8,128)} async-done(((f32[1536,768]{1,0:T(8,128)}), f32[384,768]{1,0:T(8,128)}) %reduce-scatter.9.cloned.1.call-update) | async-done | bytes 1179664 | tf_op jit(solution)/shard_map/reduce_scatter | solution.py:92
  470.3 4.1 all-to-all-start.2
  474.4 8.0 %fusion.101 = bf16[1,4,32,1536]{3,2,1,0:T(8,128)(2,1)} fusion(f32[1,10,32,1536]{3,2,1,0:T(8,128)S(1)} %maximum_convert_fusion.1, bf16[1,4,32,1536]{3,2,1,0:T(8,128)(2,1)S(1)} %copy-done.4, f32[1536]{0:T(1024)} %copy-done.17, f32[1536]{0:T(1024)} %copy-done.18, f32[1536]{0:T(1024)} %copy-done.20, f32[1536]{0:T(1024)} %copy-done.21, f32[1536]{0:T(1024)} %copy-done.22, ...), kind=kLoop, calls=%fused_computation.191 | loop fusion | flops 19660800 | bytes 8562688 | tf_op jit(solution)/shard_map/convert_element_type | solution.py:120
  482.4 2.4 copy.31
  484.8 5.2 all-to-all-done.2
  490.0 1.1 copy.30
  491.1 112.3 %all-reduce.5.cloned.1.call-done = f32[7,7,1536]{2,1,0:T(8,128)} async-done(((f32[7,7,1536]{2,1,0:T(8,128)}), f32[7,7,1536]{2,1,0:T(8,128)}) %all-reduce.5.cloned.1.call-update) | async-done | bytes 301072 | tf_op jit(solution)/shard_map/psum | solution.py:121
  603.5 1.7 copy.44
  (199 shorter events, 19.5 us)
Async XLA Ops:
  7.2 14.3 %copy-start = (bf16[1,4,32,1536]{3,2,1,0:T(8,128)(2,1)S(1)}, bf16[1,4,32,1536]{3,2,1,0:T(8,128)(2,1)}, u32[]{:S(2)}) copy-start(bf16[1,4,32,1536]{3,2,1,0:T(8,128)(2,1)} %param.7) | copy-start | bytes 1179652
  7.2 18.9 %copy-start.6 = (f32[7,7,1536]{2,1,0:T(8,128)S(1)}, f32[7,7,1536]{2,1,0:T(8,128)}, u32[]{:S(2)}) copy-start(f32[7,7,1536]{2,1,0:T(8,128)} %param.8) | copy-start | bytes 903172
  7.2 120.2 %all-gather.6.cloned.1.call-start = ((), (), s32[]{:S(2)}) async-start(), calls=%async_computation.9 | async-start | bytes 2949120 | tf_op jit(solution)/shard_map/all_gather | solution.py:42
  21.4 106.0 %all-gather.4.cloned.1.call-start = ((), (), s32[]{:S(2)}) async-start(), calls=%async_computation.8 | async-start | bytes 3538944 | tf_op jit(solution)/shard_map/all_gather | solution.py:70
  21.5 6.3 %collective-permute-start = (bf16[1,3,32,1536]{3,2,1,0:T(8,128)(2,1)S(1)}, bf16[1,3,32,1536]{3,2,1,0:T(8,128)(2,1)S(1)}, u32[]{:S(2)}, u32[]{:S(2)}) collective-permute-start(bf16[1,3,32,1536]{3,2,1,0:T(8,128)(2,1)S(1)} %get-tuple-element.118), channel_id=1, source_target_pairs={{0,1},{1,2},{2,3},{4,5},{5,6},{6,7},{8,9},{9,10},{10,11},{12,13},{... | collective-permute-start | bytes 884744 | tf_op jit(solution)/shard_map/ppermute | solution.py:22
  24.2 8.0 %collective-permute-start.1 = (bf16[1,3,32,1536]{3,2,1,0:T(8,128)(2,1)S(1)}, bf16[1,3,32,1536]{3,2,1,0:T(8,128)(2,1)S(1)}, u32[]{:S(2)}, u32[]{:S(2)}) collective-permute-start(bf16[1,3,32,1536]{3,2,1,0:T(8,128)(2,1)S(1)} %get-tuple-element.119), channel_id=1, source_target_pairs={{1,0},{2,1},{3,2},{5,4},{6,5},{7,6},{9,8},{10,9},{11,10},{13,12},{... | collective-permute-start | bytes 884744 | tf_op jit(solution)/shard_map/ppermute | solution.py:23
  26.3 6.1 copy-start.8
  26.3 6.1 copy-start.10
  26.3 6.1 copy-start.11
  26.3 6.1 copy-start.12
  26.3 6.1 copy-start.13
  26.3 6.1 copy-start.14
  26.4 6.1 copy-start.15
  26.4 6.1 copy-start.16
  26.4 6.1 copy-start.17
  26.4 6.1 copy-start.18
  26.7 5.7 copy-start.19
  26.7 5.7 copy-start.20
  26.7 5.7 copy-start.21
  26.7 5.7 copy-start.22
  26.8 5.7 copy-start.23
  26.8 5.7 copy-start.24
  26.8 5.7 copy-start.25
  26.8 5.7 copy-start.26
  26.8 5.7 copy-start.27
  32.7 9.9 %copy-start.7 = (f32[1536]{0:T(1024)S(1)}, f32[1536]{0:T(1024)}, u32[]{:S(2)}) copy-start(f32[1536]{0:T(1024)} %param.9) | copy-start | bytes 18436
  42.3 75.9 %copy-start.48 = (f32[128]{0:T(128)}, f32[128]{0:T(128)S(1)}, u32[]{:S(2)}) copy-start(f32[128]{0:T(128)S(1)} %div.15) | copy-start | bytes 1540
  42.6 75.6 %copy-start.50 = (f32[128]{0:T(128)}, f32[128]{0:T(128)S(1)}, u32[]{:S(2)}) copy-start(f32[128]{0:T(128)S(1)} %rsqrt.12) | copy-start | bytes 1540
  43.6 144.3 %reduce-scatter.5.cloned.1.call-start = ((), (), s32[]{:S(2)}) async-start(), calls=%async_computation.10 | async-start | bytes 3538944 | tf_op jit(solution)/shard_map/reduce_scatter | solution.py:74
  54.4 30.4 %collective-permute-start.2 = (bf16[768,384]{0,1:T(8,128)(2,1)S(1)}, bf16[768,384]{0,1:T(8,128)(2,1)S(1)}, u32[]{:S(2)}, u32[]{:S(2)}) collective-permute-start(bf16[768,384]{0,1:T(8,128)(2,1)S(1)} %bitcast.106), channel_id=1, source_target_pairs={{0,8},{8,16},{16,24},{24,0},{1,9},{9,17},{17,25},{25,1},{2,10},{10... | collective-permute-start | bytes 1769480 | tf_op jit(solution)/shard_map/ppermute | solution.py:46
  85.6 15.7 %collective-permute-start.3 = (bf16[768,384]{0,1:T(8,128)(2,1)S(1)}, bf16[768,384]{0,1:T(8,128)(2,1)}, u32[]{:S(2)}, u32[]{:S(2)}) collective-permute-start(bf16[768,384]{0,1:T(8,128)(2,1)S(1)} %collective-permute-done.2), channel_id=1, source_target_pairs={{0,8},{8,16},{16,24},{24,0},{1,9},{9,17},{17,25},{25,1},{2,10},{10... | collective-permute-start | bytes 1769480 | tf_op jit(solution)/shard_map/ppermute | solution.py:46
  101.3 15.0 %collective-permute-start.4 = (bf16[768,384]{0,1:T(8,128)(2,1)}, bf16[768,384]{0,1:T(8,128)(2,1)}, u32[]{:S(2)}, u32[]{:S(2)}) collective-permute-start(bf16[768,384]{0,1:T(8,128)(2,1)} %collective-permute-done.3), channel_id=1, source_target_pairs={{0,8},{8,16},{16,24},{24,0},{1,9},{9,17},{17,25},{25,1},{2,10},{10... | collective-permute-start | bytes 1769480 | tf_op jit(solution)/shard_map/ppermute | solution.py:46
  101.3 18.8 %copy-start.3 = (bf16[768,384]{0,1:T(8,128)(2,1)S(1)}, bf16[768,384]{0,1:T(8,128)(2,1)}, u32[]{:S(2)}) copy-start(bf16[768,384]{0,1:T(8,128)(2,1)} %copy-done.2) | copy-start | bytes 1769476
  141.3 46.6 %copy-start.1 = (bf16[1,4,32,1536]{3,2,1,0:T(8,128)(2,1)S(1)}, bf16[1,4,32,1536]{3,2,1,0:T(8,128)(2,1)}, u32[]{:S(2)}) copy-start(bf16[1,4,32,1536]{3,2,1,0:T(8,128)(2,1)} %param.7) | copy-start | bytes 1179652
  141.3 46.6 %copy-start.4 = (bf16[1,4,32,1536]{3,2,1,0:T(8,128)(2,1)S(1)}, bf16[1,4,32,1536]{3,2,1,0:T(8,128)(2,1)}, u32[]{:S(2)}) copy-start(bf16[1,4,32,1536]{3,2,1,0:T(8,128)(2,1)} %param.13) | copy-start | bytes 1179652
  141.4 82.1 %all-gather.8.cloned.1.call-start = ((), (), s32[]{:S(2)}) async-start(), calls=%async_computation.11 | async-start | bytes 3538944 | tf_op jit(solution)/shard_map/all_gather | solution.py:52
  190.6 125.2 %reduce-scatter.11.cloned.1.call-start = ((), (), s32[]{:S(2)}) async-start(), calls=%async_computation.14 | async-start | bytes 5898240 | tf_op jit(solution)/shard_map/reduce_scatter | solution.py:94
  230.7 150.9 %reduce-scatter.7.cloned.1.call-start = ((), (), s32[]{:S(2)}) async-start(), calls=%async_computation.12 | async-start | bytes 7077888 | tf_op jit(solution)/shard_map/reduce_scatter | solution.py:91
  230.8 8.1 %copy-start.52 = (bf16[1536,768]{1,0:T(8,128)(2,1)S(1)}, bf16[1536,768]{1,0:T(8,128)(2,1)}, u32[]{:S(2)}) copy-start(bf16[1536,768]{1,0:T(8,128)(2,1)} %all-gather.6.cloned.1.call-done) | copy-start | bytes 7077892
  243.5 226.8 %reduce-scatter.9.cloned.1.call-start = ((), (), s32[]{:S(2)}) async-start(), calls=%async_computation.13 | async-start | bytes 5898240 | tf_op jit(solution)/shard_map/reduce_scatter | solution.py:92
  250.8 130.8 %copy-start.49 = (f32[128]{0:T(128)S(1)}, f32[128]{0:T(128)}, u32[]{:S(2)}) copy-start(f32[128]{0:T(128)} %copy-done.48) | copy-start | bytes 1540
  250.8 130.8 %copy-start.51 = (f32[128]{0:T(128)S(1)}, f32[128]{0:T(128)}, u32[]{:S(2)}) copy-start(f32[128]{0:T(128)} %copy-done.50) | copy-start | bytes 1540
  318.4 151.9 %all-to-all-start.3 = ((f32[768,4,96]{0,2,1:T(8,128)}), f32[768,4,96]{0,2,1:T(8,128)}, u32[]{:S(2)}, u32[]{:S(2)}) async-start(f32[768,4,96]{0,2,1:T(8,128)} %bitcast.109), calls=%async_computation.7 | async-start | bytes 2359296 | tf_op jit(solution)/shard_map/all_to_all | solution.py:95
  323.3 280.2 %all-reduce.5.cloned.1.call-start = ((), (), s32[]{:S(2)}) async-start(), calls=%async_computation.15 | async-start | bytes 688128 | tf_op jit(solution)/shard_map/psum | solution.py:121
  401.6 58.2 %collective-permute-start.5 = (bf16[1,3,32,1536]{3,2,1,0:T(8,128)(2,1)}, bf16[1,3,32,1536]{3,2,1,0:T(8,128)(2,1)S(1)}, u32[]{:S(2)}, u32[]{:S(2)}) collective-permute-start(bf16[1,3,32,1536]{3,2,1,0:T(8,128)(2,1)} %get-tuple-element.116), channel_id=1, source_target_pairs={{0,1},{1,2},{2,3},{4,5},{5,6},{6,7},{8,9},{9,10},{10,11},{12,13},{... | collective-permute-start | bytes 884744 | tf_op jit(solution)/shard_map/ppermute | solution.py:22
  405.2 54.6 %collective-permute-start.6 = (bf16[1,3,32,1536]{3,2,1,0:T(8,128)(2,1)}, bf16[1,3,32,1536]{3,2,1,0:T(8,128)(2,1)}, u32[]{:S(2)}, u32[]{:S(2)}) collective-permute-start(bf16[1,3,32,1536]{3,2,1,0:T(8,128)(2,1)} %get-tuple-element.117), channel_id=1, source_target_pairs={{1,0},{2,1},{3,2},{5,4},{6,5},{7,6},{9,8},{10,9},{11,10},{13,12},{... | collective-permute-start | bytes 884744 | tf_op jit(solution)/shard_map/ppermute | solution.py:23
  459.8 14.6 %copy-start.9 = (f32[1536]{0:T(1024)S(1)}, f32[1536]{0:T(1024)}, u32[]{:S(2)}) copy-start(f32[1536]{0:T(1024)} %copy-done.8) | copy-start | bytes 18436
  470.3 19.7 %all-to-all-start.2 = ((f32[4,96,768]{2,1,0:T(8,128)}), f32[4,96,768]{2,1,0:T(8,128)S(1)}, u32[]{:S(2)}, u32[]{:S(2)}) async-start(f32[4,96,768]{2,1,0:T(8,128)} %bitcast.115), calls=%async_computation.5 | async-start | bytes 2359296 | tf_op jit(solution)/shard_map/all_to_all | solution.py:93
  (23 other events, 109.5 us)
Sparse Core Ops, SparseCore 0:
  21.5 63.6 all-gather.5
  87.7 31.6 all-gather.3
  141.5 46.3 reduce-scatter.4
  190.7 32.6 all-gather.7
  230.8 84.8 reduce-scatter.10
  319.4 62.1 reduce-scatter.6
  383.9 86.3 reduce-scatter.8
  476.2 127.2 all-reduce.4
